TPU v7x, 512 devices: a whole 4x8x8 slice. The times are simulated.
512 devices in a mesh: ctx: 32 (over z, x), exp: 16 (over y, core).
Axes of the slice: x: 4, y: 8, z: 8, core: 2. Of those that a mesh axis runs over, the one named last changes fastest.
Arguments:
- stream: bfloat16 [16, 4096, 1024], P('exp', 'ctx'), may hold values from -400 to 400
- queries: bfloat16 [16, 4096, 16, 128], P('exp', 'ctx'), may hold values from -6 to 6
- key_rows: bfloat16 [16, 4096, 2, 128], P('exp', 'ctx'), may hold values from -4 to 4
- value_rows: bfloat16 [16, 4096, 2, 128], P('exp', 'ctx'), may hold values from -6 to 6
- expert_ids: int32 [16, 4096, 2], P('exp', 'ctx'), may hold values from 0 to 127, as said below
- norm_gain: bfloat16 [1024], replicated, may hold values from 0.099609375 to 1.8984375
- router_weight: bfloat16 [1024, 128], replicated, may hold values from -0.1875 to 0.1875
- gate_weight: bfloat16 [98304, 1024], P(('ctx', 'exp')), may hold values from -0.1875 to 0.1875
- up_weight: bfloat16 [98304, 1024], P(('ctx', 'exp')), may hold values from -0.1875 to 0.1875
- down_weight: bfloat16 [98304, 1024], P(('ctx', 'exp')), may hold values from -0.21875 to 0.21875
Outputs:
- attended: bfloat16 [16, 4096, 16, 128], P('exp', 'ctx')
- expert_mix: bfloat16 [16, 4096, 1024], P('exp', 'ctx')
Inputs may be any that keep to these rules, and one draw needn't show every extreme that they name: `expert_ids`: within the rows of one device (aligned blocks of 128 positions of one sequence), a token's 2 experts differ and no expert is named more than 4 times; one expert is named exactly 4 times in every such block.
All inputs are finite; a program needn't handle non-finite values.
Results may differ from a plain program's by a relative error of at most 0.01.
Values may be sent and summed in bfloat16 or wider, within the bound.
No kernel may reach another device: no remote copies, remote signals or barrier semaphores. Data moves between devices by JAX's collectives and lax.ppermute only.
A program may use at most 64 MiB of HBM per device.

v0:
```python
import math
import jax
import jax.numpy as jnp
from jax import lax
from jax.sharding import PartitionSpec as P


def from_partner(value, axis, bit):
    return lax.ppermute(value, axis, [(i, i ^ 1 << bit) for i in range(lax.axis_size(axis))])


def expert_rows(inputs, gate_rows, up_rows, down_rows):
    features = inputs.shape[-1]
    flat_rows = inputs.reshape(-1, features)
    contract = (((1,), (1,)), ((), ()))
    gate_part = lax.dot_general(flat_rows, gate_rows, contract, preferred_element_type=jnp.float32)
    up_part = lax.dot_general(flat_rows, up_rows, contract, preferred_element_type=jnp.float32)
    hidden = (jax.nn.silu(gate_part) * up_part).astype(jnp.bfloat16)
    projected = jnp.dot(hidden, down_rows, preferred_element_type=jnp.float32)
    return projected.reshape(inputs.shape)


def attention(queries, key_rows, value_rows):
    seq_rows = queries.shape[1]
    head_count = queries.shape[2]
    head_size = queries.shape[3]
    kv_count = key_rows.shape[2]
    group_size = head_count // kv_count
    grouped = queries[0].reshape(seq_rows, kv_count, group_size, head_size)
    scaling = 1.0 / math.sqrt(head_size)
    query_pos = lax.axis_index("ctx") * seq_rows + jnp.arange(seq_rows, dtype=jnp.int32)
    initial = (
        jnp.full((kv_count, group_size, seq_rows), -1e30, jnp.float32),
        jnp.zeros((kv_count, group_size, seq_rows), jnp.float32),
        jnp.zeros((kv_count, group_size, seq_rows, head_size), jnp.float32),
    )
    key_piece = lax.all_gather(key_rows, "ctx", axis=1, tiled=True)
    value_piece = lax.all_gather(value_rows, "ctx", axis=1, tiled=True)
    piece_rows = key_piece.shape[1]
    block_rows = math.gcd(piece_rows, 512)
    block_count = piece_rows // block_rows
    key_blocks = key_piece[0].reshape(block_count, block_rows, kv_count, head_size)
    value_blocks = value_piece[0].reshape(block_count, block_rows, kv_count, head_size)

    def advance(status, members):
        running, totals, accumulated = status
        key_block, value_block, offset = members
        scores = (
            jnp.einsum("qhgd,khd->hgqk", grouped, key_block, preferred_element_type=jnp.float32)
            * scaling
        )
        key_pos = offset * block_rows + jnp.arange(block_rows, dtype=jnp.int32)
        visible = key_pos[None, :] <= query_pos[:, None]
        scores = jnp.where(visible, scores, -1e30)
        highest = jnp.maximum(running, jnp.max(scores, axis=-1))
        factor = jnp.exp(running - highest)
        weights = jnp.where(visible, jnp.exp(scores - highest[..., None]), 0.0)
        totals = totals * factor + jnp.sum(weights, axis=-1)
        accumulated = accumulated * factor[..., None] + jnp.einsum(
            "hgqk,khd->hgqd",
            weights.astype(jnp.bfloat16),
            value_block,
            preferred_element_type=jnp.float32,
        )
        return ((highest, totals, accumulated), None)

    status, unused = lax.scan(
        advance, initial, (key_blocks, value_blocks, jnp.arange(block_count, dtype=jnp.int32))
    )
    running, totals, accumulated = status
    result = accumulated / totals[..., None]
    return (
        jnp.transpose(result, (2, 0, 1, 3))
        .reshape(1, seq_rows, head_count, head_size)
        .astype(jnp.bfloat16)
    )


def local(
    stream,
    queries,
    key_rows,
    value_rows,
    expert_ids,
    norm_gain,
    router_weight,
    gate_weight,
    up_weight,
    down_weight,
):
    attended = attention(queries, key_rows, value_rows)
    ctx_count = lax.axis_size("ctx")
    exp_count = lax.axis_size("exp")
    tokens = stream.shape[1]
    features = stream.shape[2]
    top_count = expert_ids.shape[2]
    expert_total = router_weight.shape[1]
    per_ctx = expert_total // ctx_count
    quarters = exp_count // per_ctx
    capacity = 2 * tokens * top_count // expert_total
    widened = stream[0].astype(jnp.float32)
    mean_square = jnp.mean(widened * widened, axis=-1, keepdims=True)
    normed = (widened * lax.rsqrt(mean_square + 1e-06) * norm_gain.astype(jnp.float32)).astype(
        jnp.bfloat16
    )
    logits = jnp.dot(normed, router_weight, preferred_element_type=jnp.float32)
    chosen = expert_ids[0]
    gate_values = jax.nn.sigmoid(jnp.take_along_axis(logits, chosen, axis=1))
    flat_ids = chosen.reshape(-1)
    onehot = (flat_ids[:, None] == jnp.arange(expert_total, dtype=jnp.int32)[None, :]).astype(
        jnp.int32
    )
    earlier = jnp.cumsum(onehot, axis=0) - onehot
    slot_index = jnp.sum(earlier * onehot, axis=1)
    target = (flat_ids % per_ctx * ctx_count + flat_ids // per_ctx) * capacity + slot_index
    source_rows = jnp.repeat(normed, top_count, axis=0)
    outgoing = (
        jnp.zeros((expert_total * capacity, features), jnp.bfloat16).at[target].set(source_rows)
    )
    outgoing = outgoing.reshape(per_ctx, ctx_count, capacity, features)
    arrived = lax.all_to_all(outgoing, "ctx", split_axis=1, concat_axis=1, tiled=True)
    stacked = jnp.stack([gate_weight, up_weight, down_weight], axis=0)
    my_exp = lax.axis_index("exp")
    partner = from_partner(stacked, "exp", 0)
    upper_side = my_exp & 1 == 1
    held = jnp.where(
        upper_side,
        jnp.concatenate([partner, stacked], axis=1),
        jnp.concatenate([stacked, partner], axis=1),
    )
    half_ctx = ctx_count // 2
    halves_rows = arrived.reshape(per_ctx, 1, 2, half_ctx, capacity, features)
    spread_rows = jnp.broadcast_to(
        halves_rows, (per_ctx, quarters // 2, 2, half_ctx, capacity, features)
    )
    spread_rows = spread_rows.reshape(exp_count, half_ctx, capacity, features)
    received = lax.all_to_all(spread_rows, "exp", split_axis=0, concat_axis=0, tiled=True)
    partials = expert_rows(received, held[0], held[1], held[2])
    returned = lax.all_to_all(
        partials.astype(jnp.bfloat16), "exp", split_axis=0, concat_axis=0, tiled=True
    ).astype(partials.dtype)
    summed = jnp.sum(
        returned.reshape(per_ctx, quarters // 2, 2, half_ctx, capacity, features), axis=1
    )
    finished = summed.astype(jnp.bfloat16).reshape(per_ctx, ctx_count, capacity, features)
    came_back = lax.all_to_all(finished, "ctx", split_axis=1, concat_axis=1, tiled=True)
    flat_back = came_back.reshape(expert_total * capacity, features)
    picked = (
        jnp.take(flat_back, target, axis=0).astype(jnp.float32).reshape(tokens, top_count, features)
    )
    mixture = jnp.sum(picked * gate_values[:, :, None], axis=1).astype(jnp.bfloat16)
    return (attended, mixture[None])


def solution(mesh):
    placed = (
        P("exp", "ctx", None),
        P("exp", "ctx", None, None),
        P("exp", "ctx", None, None),
        P("exp", "ctx", None, None),
        P("exp", "ctx", None),
        P(),
        P(),
        P(("ctx", "exp"), None),
        P(("ctx", "exp"), None),
        P(("ctx", "exp"), None),
    )
    return jax.shard_map(
        local,
        mesh=mesh,
        in_specs=placed,
        out_specs=(P("exp", "ctx", None, None), P("exp", "ctx", None)),
        check_vma=False,
    )
```

profile of v0, /device:TPU:16, one launch (start us, length us, event | category | flops | bytes accessed | tf_op | source)
XLA Modules:
  0.0 309.8 jit_solution(2212090198150793443)
XLA Ops:
  12.4 1.9 scatter_custom_fusion
  16.4 13.2 %all-to-all-start = ((bf16[4,32,4,1024]{3,2,0,1:T(4,128)(2,1)}), bf16[4,32,4,1024]{3,2,0,1:T(4,128)(2,1)S(1)}, u32[]{:S(2)}, u32[]{:S(2)}) async-start(bf16[4,32,4,1024]{3,2,0,1:T(4,128)(2,1)} %copy.84), calls=%async_computation | async-start | bytes 2097152 | tf_op jit(solution)/shard_map/all_to_all | solution.py:121
  30.3 27.4 %all-to-all-done = bf16[4,32,4,1024]{3,2,0,1:T(4,128)(2,1)S(1)} async-done(((bf16[4,32,4,1024]{3,2,0,1:T(4,128)(2,1)}), bf16[4,32,4,1024]{3,2,0,1:T(4,128)(2,1)S(1)}, u32[]{:S(2)}, u32[]{:S(2)}) %all-to-all-start) | async-done | bytes 1048608 | tf_op jit(solution)/shard_map/all_to_all | solution.py:121
  58.1 2.1 broadcast_in_dim.66
  60.2 7.6 %all-to-all-start.1 = ((bf16[16,16,4,1024]{3,2,1,0:T(4,128)(2,1)}), bf16[16,16,4,1024]{3,2,1,0:T(4,128)(2,1)S(1)}, u32[]{:S(2)}, u32[]{:S(2)}) async-start(bf16[16,16,4,1024]{3,2,1,0:T(4,128)(2,1)} %bitcast.120), calls=%async_computation.1 | async-start | bytes 4194304 | tf_op jit(solution)/shard_map/all_to_all | solution.py:137
  67.8 2.2 pad_maximum_fusion
  70.0 2.0 collective-permute-start
  72.7 2.3 collective-permute-done
  75.1 3.5 %maximum_select_fusion = bf16[3,384,1024]{2,1,0:T(8,128)(2,1)} fusion(bf16[1,192,1024]{2,1,0:T(8,128)(2,1)S(1)} %bitcast.124, bf16[1,192,1024]{2,1,0:T(8,128)(2,1)S(1)} %bitcast.126, bf16[1,192,1024]{2,1,0:T(8,128)(2,1)} %bitcast.128, bf16[3,192,1024]{2,1,0:T(8,128)(2,1)} %collective-permute-done, pred[]{:T(512)S(6)} %eq.35), kind=kLoop, calls=%fused_computation.30 | loop fusion | flops 20054016 | bytes 4718593 | tf_op jit(solution)/shard_map/jit(_where)/select_n | solution.py:126
  78.6 36.6 %all-to-all-done.1 = bf16[16,16,4,1024]{3,2,1,0:T(4,128)(2,1)S(1)} async-done(((bf16[16,16,4,1024]{3,2,1,0:T(4,128)(2,1)}), bf16[16,16,4,1024]{3,2,1,0:T(4,128)(2,1)S(1)}, u32[]{:S(2)}, u32[]{:S(2)}) %all-to-all-start.1) | async-done | bytes 2097184 | tf_op jit(solution)/shard_map/all_to_all | solution.py:137
  115.2 2.0 reshape.284
  117.2 3.2 %fusion.22 = f32[1024,384]{1,0:T(8,128)S(1)} fusion(bf16[1024,1024]{1,0:T(8,128)(2,1)} %reshape.284, bf16[3,384,1024]{2,1,0:T(8,128)(2,1)} %maximum_select_fusion), kind=kOutput, calls=%fused_computation.40 | convolution fusion | flops 805306368 | bytes 4456448 | tf_op jit(solution)/shard_map/dot_general | solution.py:16
  120.4 2.3 multiply_convert_fusion
  122.7 2.4 dot_general.22
  125.1 3.7 %convolution_convert_fusion = bf16[16,16,4,1024]{3,1,2,0:T(8,128)(2,1)} fusion(bf16[3,384,1024]{2,1,0:T(8,128)(2,1)S(1)} %copy-done.2, bf16[16,16,4,384]{3,2,1,0:T(4,128)(2,1)} %dot_general.22), kind=kOutput, calls=%fused_computation.31 | convolution fusion | flops 806354944 | bytes 3670016 | tf_op jit(solution)/shard_map/dot_general | solution.py:19
  128.8 6.7 %all-to-all-start.2 = ((bf16[16,16,4,1024]{3,1,2,0:T(8,128)(2,1)}), bf16[16,16,4,1024]{3,1,2,0:T(8,128)(2,1)S(1)}, u32[]{:S(2)}, u32[]{:S(2)}) async-start(bf16[16,16,4,1024]{3,1,2,0:T(8,128)(2,1)} %convolution_convert_fusion), calls=%async_computation.2 | async-start | bytes 4194304 | tf_op jit(solution)/shard_map/all_to_all | solution.py:139
  137.6 1.9 gather_fusion.1
  139.9 43.0 %all-to-all-done.2 = bf16[16,16,4,1024]{3,1,2,0:T(8,128)(2,1)S(1)} async-done(((bf16[16,16,4,1024]{3,1,2,0:T(8,128)(2,1)}), bf16[16,16,4,1024]{3,1,2,0:T(8,128)(2,1)S(1)}, u32[]{:S(2)}, u32[]{:S(2)}) %all-to-all-start.2) | async-done | bytes 2097184 | tf_op jit(solution)/shard_map/all_to_all | solution.py:139
  182.8 1.8 reduce
  185.9 1.8 copy.88
  187.7 5.3 %all-to-all-start.3 = ((bf16[4,32,4,1024]{3,2,0,1:T(4,128)(2,1)}), bf16[4,32,4,1024]{3,2,0,1:T(4,128)(2,1)S(1)}, u32[]{:S(2)}, u32[]{:S(2)}) async-start(bf16[4,32,4,1024]{3,2,0,1:T(4,128)(2,1)} %copy.88), calls=%async_computation.3 | async-start | bytes 2097152 | tf_op jit(solution)/shard_map/all_to_all | solution.py:146
  193.1 14.3 %all-gather.5.cloned.1.call-done = bf16[1,4096,2,128]{3,1,2,0:T(8,128)(2,1)} async-done(((bf16[1,128,2,128]{3,1,2,0:T(8,128)(2,1)}), bf16[1,4096,2,128]{3,1,2,0:T(8,128)(2,1)}) %all-gather.5.cloned.1.call-update) | async-done | bytes 2097168 | tf_op jit(solution)/shard_map/all_gather | solution.py:38
  207.4 89.6 %while.15 = (s32[]{:T(128)}, f32[2,8,128]{2,1,0:T(8,128)S(1)}, f32[2,8,128]{2,1,0:T(8,128)S(1)}, f32[2,8,128,128]{3,2,1,0:T(8,128)S(1)}, s32[8]{0:T(128)S(1)}, /...) while((s32[]{:T(128)}, f32[2,8,128]{2,1,0:T(8,128)S(1)}, ...), condition=%wide.region_3.4_spmd.clone, body=%wide.region_0.3_spmd.clone.sunk | while | flops 551365248 | bytes 32904396 | solution.py:67
  208.8 3.7 %fusion.58 = (f32[2,8,128]{2,1,0:T(8,128)S(1)}, f32[2,512,128,8]{2,1,3,0:T(8,128)}) fusion(pred[128,512]{0,1:T(8,128)(4,1)S(1)} %broadcast_compare_fusion.2, bf16[128,2,8,128]{3,0,2,1:T(8,128)(2,1)S(1)} %get-tuple-element.236, bf16[8,512,2,128]{3,1,0,2:T(8,128)(2,1)} %get-tuple-element.235, s32[]{:T(128)S(6)} %copy.107), kind=kOutput, calls=%fused_computation.6.clone.1 | convolution fusion | flops 271579136 | bytes 5054468 | tf_op jit(solution)/shard_map/while/body/eval_jaxpr/qhgd,khd->hgqk/dot_general | solution.py:49
  212.5 3.3 %fusion.59 = f32[2,8,128]{2,1,0:T(8,128)S(1)} fusion(f32[2,512,128,8]{2,1,3,0:T(8,128)} %get-tuple-element.203, f32[2,8,128]{2,1,0:T(8,128)S(1)} %select_maximum_fusion.2, pred[128,512]{0,1:T(8,128)(4,1)S(1)} %broadcast_compare_fusion.2), kind=kLoop, calls=%fused_computation.8.clone.1 | loop fusion | flops 5240832 | bytes 4276224 | tf_op jit(solution)/shard_map/while/body/eval_jaxpr/reduce_sum | solution.py:58
  216.0 2.6 fusion.61
  220.0 3.7 %fusion.58 = (f32[2,8,128]{2,1,0:T(8,128)S(1)}, f32[2,512,128,8]{2,1,3,0:T(8,128)}) fusion(pred[128,512]{0,1:T(8,128)(4,1)S(1)} %broadcast_compare_fusion.2, bf16[128,2,8,128]{3,0,2,1:T(8,128)(2,1)S(1)} %get-tuple-element.236, bf16[8,512,2,128]{3,1,0,2:T(8,128)(2,1)} %get-tuple-element.235, s32[]{:T(128)S(6)} %copy.107), kind=kOutput, calls=%fused_computation.6.clone.1 | convolution fusion | flops 271579136 | bytes 5054468 | tf_op jit(solution)/shard_map/while/body/eval_jaxpr/qhgd,khd->hgqk/dot_general | solution.py:49
  223.7 3.3 %fusion.59 = f32[2,8,128]{2,1,0:T(8,128)S(1)} fusion(f32[2,512,128,8]{2,1,3,0:T(8,128)} %get-tuple-element.203, f32[2,8,128]{2,1,0:T(8,128)S(1)} %select_maximum_fusion.2, pred[128,512]{0,1:T(8,128)(4,1)S(1)} %broadcast_compare_fusion.2), kind=kLoop, calls=%fused_computation.8.clone.1 | loop fusion | flops 5240832 | bytes 4276224 | tf_op jit(solution)/shard_map/while/body/eval_jaxpr/reduce_sum | solution.py:58
  227.2 2.6 fusion.61
  231.2 3.7 %fusion.58 = (f32[2,8,128]{2,1,0:T(8,128)S(1)}, f32[2,512,128,8]{2,1,3,0:T(8,128)}) fusion(pred[128,512]{0,1:T(8,128)(4,1)S(1)} %broadcast_compare_fusion.2, bf16[128,2,8,128]{3,0,2,1:T(8,128)(2,1)S(1)} %get-tuple-element.236, bf16[8,512,2,128]{3,1,0,2:T(8,128)(2,1)} %get-tuple-element.235, s32[]{:T(128)S(6)} %copy.107), kind=kOutput, calls=%fused_computation.6.clone.1 | convolution fusion | flops 271579136 | bytes 5054468 | tf_op jit(solution)/shard_map/while/body/eval_jaxpr/qhgd,khd->hgqk/dot_general | solution.py:49
  234.9 3.3 %fusion.59 = f32[2,8,128]{2,1,0:T(8,128)S(1)} fusion(f32[2,512,128,8]{2,1,3,0:T(8,128)} %get-tuple-element.203, f32[2,8,128]{2,1,0:T(8,128)S(1)} %select_maximum_fusion.2, pred[128,512]{0,1:T(8,128)(4,1)S(1)} %broadcast_compare_fusion.2), kind=kLoop, calls=%fused_computation.8.clone.1 | loop fusion | flops 5240832 | bytes 4276224 | tf_op jit(solution)/shard_map/while/body/eval_jaxpr/reduce_sum | solution.py:58
  238.4 2.6 fusion.61
  242.5 3.7 %fusion.58 = (f32[2,8,128]{2,1,0:T(8,128)S(1)}, f32[2,512,128,8]{2,1,3,0:T(8,128)}) fusion(pred[128,512]{0,1:T(8,128)(4,1)S(1)} %broadcast_compare_fusion.2, bf16[128,2,8,128]{3,0,2,1:T(8,128)(2,1)S(1)} %get-tuple-element.236, bf16[8,512,2,128]{3,1,0,2:T(8,128)(2,1)} %get-tuple-element.235, s32[]{:T(128)S(6)} %copy.107), kind=kOutput, calls=%fused_computation.6.clone.1 | convolution fusion | flops 271579136 | bytes 5054468 | tf_op jit(solution)/shard_map/while/body/eval_jaxpr/qhgd,khd->hgqk/dot_general | solution.py:49
  246.1 3.3 %fusion.59 = f32[2,8,128]{2,1,0:T(8,128)S(1)} fusion(f32[2,512,128,8]{2,1,3,0:T(8,128)} %get-tuple-element.203, f32[2,8,128]{2,1,0:T(8,128)S(1)} %select_maximum_fusion.2, pred[128,512]{0,1:T(8,128)(4,1)S(1)} %broadcast_compare_fusion.2), kind=kLoop, calls=%fused_computation.8.clone.1 | loop fusion | flops 5240832 | bytes 4276224 | tf_op jit(solution)/shard_map/while/body/eval_jaxpr/reduce_sum | solution.py:58
  249.6 2.6 fusion.61
  253.7 3.7 %fusion.58 = (f32[2,8,128]{2,1,0:T(8,128)S(1)}, f32[2,512,128,8]{2,1,3,0:T(8,128)}) fusion(pred[128,512]{0,1:T(8,128)(4,1)S(1)} %broadcast_compare_fusion.2, bf16[128,2,8,128]{3,0,2,1:T(8,128)(2,1)S(1)} %get-tuple-element.236, bf16[8,512,2,128]{3,1,0,2:T(8,128)(2,1)} %get-tuple-element.235, s32[]{:T(128)S(6)} %copy.107), kind=kOutput, calls=%fused_computation.6.clone.1 | convolution fusion | flops 271579136 | bytes 5054468 | tf_op jit(solution)/shard_map/while/body/eval_jaxpr/qhgd,khd->hgqk/dot_general | solution.py:49
  257.3 3.3 %fusion.59 = f32[2,8,128]{2,1,0:T(8,128)S(1)} fusion(f32[2,512,128,8]{2,1,3,0:T(8,128)} %get-tuple-element.203, f32[2,8,128]{2,1,0:T(8,128)S(1)} %select_maximum_fusion.2, pred[128,512]{0,1:T(8,128)(4,1)S(1)} %broadcast_compare_fusion.2), kind=kLoop, calls=%fused_computation.8.clone.1 | loop fusion | flops 5240832 | bytes 4276224 | tf_op jit(solution)/shard_map/while/body/eval_jaxpr/reduce_sum | solution.py:58
  260.8 2.6 fusion.61
  264.9 3.7 %fusion.58 = (f32[2,8,128]{2,1,0:T(8,128)S(1)}, f32[2,512,128,8]{2,1,3,0:T(8,128)}) fusion(pred[128,512]{0,1:T(8,128)(4,1)S(1)} %broadcast_compare_fusion.2, bf16[128,2,8,128]{3,0,2,1:T(8,128)(2,1)S(1)} %get-tuple-element.236, bf16[8,512,2,128]{3,1,0,2:T(8,128)(2,1)} %get-tuple-element.235, s32[]{:T(128)S(6)} %copy.107), kind=kOutput, calls=%fused_computation.6.clone.1 | convolution fusion | flops 271579136 | bytes 5054468 | tf_op jit(solution)/shard_map/while/body/eval_jaxpr/qhgd,khd->hgqk/dot_general | solution.py:49
  268.6 3.3 %fusion.59 = f32[2,8,128]{2,1,0:T(8,128)S(1)} fusion(f32[2,512,128,8]{2,1,3,0:T(8,128)} %get-tuple-element.203, f32[2,8,128]{2,1,0:T(8,128)S(1)} %select_maximum_fusion.2, pred[128,512]{0,1:T(8,128)(4,1)S(1)} %broadcast_compare_fusion.2), kind=kLoop, calls=%fused_computation.8.clone.1 | loop fusion | flops 5240832 | bytes 4276224 | tf_op jit(solution)/shard_map/while/body/eval_jaxpr/reduce_sum | solution.py:58
  272.0 2.6 fusion.61
  276.1 3.7 %fusion.58 = (f32[2,8,128]{2,1,0:T(8,128)S(1)}, f32[2,512,128,8]{2,1,3,0:T(8,128)}) fusion(pred[128,512]{0,1:T(8,128)(4,1)S(1)} %broadcast_compare_fusion.2, bf16[128,2,8,128]{3,0,2,1:T(8,128)(2,1)S(1)} %get-tuple-element.236, bf16[8,512,2,128]{3,1,0,2:T(8,128)(2,1)} %get-tuple-element.235, s32[]{:T(128)S(6)} %copy.107), kind=kOutput, calls=%fused_computation.6.clone.1 | convolution fusion | flops 271579136 | bytes 5054468 | tf_op jit(solution)/shard_map/while/body/eval_jaxpr/qhgd,khd->hgqk/dot_general | solution.py:49
  279.8 3.3 %fusion.59 = f32[2,8,128]{2,1,0:T(8,128)S(1)} fusion(f32[2,512,128,8]{2,1,3,0:T(8,128)} %get-tuple-element.203, f32[2,8,128]{2,1,0:T(8,128)S(1)} %select_maximum_fusion.2, pred[128,512]{0,1:T(8,128)(4,1)S(1)} %broadcast_compare_fusion.2), kind=kLoop, calls=%fused_computation.8.clone.1 | loop fusion | flops 5240832 | bytes 4276224 | tf_op jit(solution)/shard_map/while/body/eval_jaxpr/reduce_sum | solution.py:58
  283.2 2.6 fusion.61
  287.3 3.7 %fusion.58 = (f32[2,8,128]{2,1,0:T(8,128)S(1)}, f32[2,512,128,8]{2,1,3,0:T(8,128)}) fusion(pred[128,512]{0,1:T(8,128)(4,1)S(1)} %broadcast_compare_fusion.2, bf16[128,2,8,128]{3,0,2,1:T(8,128)(2,1)S(1)} %get-tuple-element.236, bf16[8,512,2,128]{3,1,0,2:T(8,128)(2,1)} %get-tuple-element.235, s32[]{:T(128)S(6)} %copy.107), kind=kOutput, calls=%fused_computation.6.clone.1 | convolution fusion | flops 271579136 | bytes 5054468 | tf_op jit(solution)/shard_map/while/body/eval_jaxpr/qhgd,khd->hgqk/dot_general | solution.py:49
  291.0 3.3 %fusion.59 = f32[2,8,128]{2,1,0:T(8,128)S(1)} fusion(f32[2,512,128,8]{2,1,3,0:T(8,128)} %get-tuple-element.203, f32[2,8,128]{2,1,0:T(8,128)S(1)} %select_maximum_fusion.2, pred[128,512]{0,1:T(8,128)(4,1)S(1)} %broadcast_compare_fusion.2), kind=kLoop, calls=%fused_computation.8.clone.1 | loop fusion | flops 5240832 | bytes 4276224 | tf_op jit(solution)/shard_map/while/body/eval_jaxpr/reduce_sum | solution.py:58
  294.4 2.6 fusion.61
  300.6 2.3 multiply_reduce_fusion
  (146 shorter events, 23.0 us)
Async XLA Ops:
  7.2 130.2 %copy-start = (bf16[1024,128]{1,0:T(8,128)(2,1)S(1)}, bf16[1024,128]{1,0:T(8,128)(2,1)}, u32[]{:S(2)}) copy-start(bf16[1024,128]{1,0:T(8,128)(2,1)} %param.18) | copy-start | bytes 786436
  14.8 14.8 %copy-start.7 = (bf16[1,128,2,128]{3,2,1,0:T(2,128)(2,1)S(1)}, bf16[1,128,2,128]{3,2,1,0:T(2,128)(2,1)}, u32[]{:S(2)}) copy-start(bf16[1,128,2,128]{3,2,1,0:T(2,128)(2,1)} %param.14) | copy-start | bytes 196612
  16.4 41.3 %all-to-all-start = ((bf16[4,32,4,1024]{3,2,0,1:T(4,128)(2,1)}), bf16[4,32,4,1024]{3,2,0,1:T(4,128)(2,1)S(1)}, u32[]{:S(2)}, u32[]{:S(2)}) async-start(bf16[4,32,4,1024]{3,2,0,1:T(4,128)(2,1)} %copy.84), calls=%async_computation | async-start | bytes 2097152 | tf_op jit(solution)/shard_map/all_to_all | solution.py:121
  29.5 163.6 %all-gather.3.cloned.1.call-start = ((), (), s32[]{:S(2)}) async-start(), calls=%async_computation.4 | async-start | bytes 2162688 | tf_op jit(solution)/shard_map/all_gather | solution.py:37
  60.2 7.6 %copy-start.4 = (bf16[192,1024]{1,0:T(8,128)(2,1)S(1)}, bf16[192,1024]{1,0:T(8,128)(2,1)}, u32[]{:S(2)}) copy-start(bf16[192,1024]{1,0:T(8,128)(2,1)} %param.21) | copy-start | bytes 1179652
  60.2 7.6 %copy-start.5 = (bf16[192,1024]{1,0:T(8,128)(2,1)S(1)}, bf16[192,1024]{1,0:T(8,128)(2,1)}, u32[]{:S(2)}) copy-start(bf16[192,1024]{1,0:T(8,128)(2,1)} %param.20) | copy-start | bytes 1179652
  60.2 11.9 %copy-start.8 = (bf16[1,128,2,128]{3,2,1,0:T(2,128)(2,1)S(1)}, bf16[1,128,2,128]{3,2,1,0:T(2,128)(2,1)}, u32[]{:S(2)}) copy-start(bf16[1,128,2,128]{3,2,1,0:T(2,128)(2,1)} %param.15) | copy-start | bytes 196612
  60.2 55.0 %all-to-all-start.1 = ((bf16[16,16,4,1024]{3,2,1,0:T(4,128)(2,1)}), bf16[16,16,4,1024]{3,2,1,0:T(4,128)(2,1)S(1)}, u32[]{:S(2)}, u32[]{:S(2)}) async-start(bf16[16,16,4,1024]{3,2,1,0:T(4,128)(2,1)} %bitcast.120), calls=%async_computation.1 | async-start | bytes 4194304 | tf_op jit(solution)/shard_map/all_to_all | solution.py:137
  67.8 139.7 %all-gather.5.cloned.1.call-start = ((), (), s32[]{:S(2)}) async-start(), calls=%async_computation.5 | async-start | bytes 2162688 | tf_op jit(solution)/shard_map/all_gather | solution.py:38
  70.0 5.1 %collective-permute-start = (bf16[3,192,1024]{2,1,0:T(8,128)(2,1)}, bf16[3,192,1024]{2,1,0:T(8,128)(2,1)}, u32[]{:S(2)}, u32[]{:S(2)}) collective-permute-start(bf16[3,192,1024]{2,1,0:T(8,128)(2,1)} %pad_maximum_fusion), channel_id=1, source_target_pairs={{0,1},{1,0},{2,3},{3,2},{4,5},{5,4},{6,7},{7,6},{8,9},{9,8},{10,11... | collective-permute-start | bytes 3538952 | tf_op jit(solution)/shard_map/ppermute | solution.py:9
  117.2 3.2 %copy-start.2 = (bf16[3,384,1024]{2,1,0:T(8,128)(2,1)S(1)}, bf16[3,384,1024]{2,1,0:T(8,128)(2,1)}, u32[]{:S(2)}) copy-start(bf16[3,384,1024]{2,1,0:T(8,128)(2,1)} %maximum_select_fusion) | copy-start | bytes 7077892
  117.2 3.2 %copy-start.3 = (bf16[1024,1024]{1,0:T(8,128)(2,1)S(1)}, bf16[1024,1024]{1,0:T(8,128)(2,1)}, u32[]{:S(2)}) copy-start(bf16[1024,1024]{1,0:T(8,128)(2,1)} %reshape.284) | copy-start | bytes 6291460
  128.8 8.1 %copy-start.9 = (s32[1,128,2]{1,2,0:T(2,128)S(1)}, s32[1,128,2]{1,2,0:T(2,128)}, u32[]{:S(2)}) copy-start(s32[1,128,2]{1,2,0:T(2,128)} %param.16) | copy-start | bytes 3076
  128.8 54.1 %all-to-all-start.2 = ((bf16[16,16,4,1024]{3,1,2,0:T(8,128)(2,1)}), bf16[16,16,4,1024]{3,1,2,0:T(8,128)(2,1)S(1)}, u32[]{:S(2)}, u32[]{:S(2)}) async-start(bf16[16,16,4,1024]{3,1,2,0:T(8,128)(2,1)} %convolution_convert_fusion), calls=%async_computation.2 | async-start | bytes 4194304 | tf_op jit(solution)/shard_map/all_to_all | solution.py:139
  185.9 21.5 %copy-start.6 = (f32[2,8,128,128]{3,2,1,0:T(8,128)S(1)}, f32[2,8,128,128]{3,2,1,0:T(8,128)}, u32[]{:S(2)}) copy-start(f32[2,8,128,128]{3,2,1,0:T(8,128)} %custom-call.4) | copy-start | bytes 3145732
  187.7 110.8 %all-to-all-start.3 = ((bf16[4,32,4,1024]{3,2,0,1:T(4,128)(2,1)}), bf16[4,32,4,1024]{3,2,0,1:T(4,128)(2,1)S(1)}, u32[]{:S(2)}, u32[]{:S(2)}) async-start(bf16[4,32,4,1024]{3,2,0,1:T(4,128)(2,1)} %copy.88), calls=%async_computation.3 | async-start | bytes 2097152 | tf_op jit(solution)/shard_map/all_to_all | solution.py:146
  212.5 3.4 %copy-start.1 = (f32[2,512,128,8]{2,1,3,0:T(8,128)S(1)}, f32[2,512,128,8]{2,1,3,0:T(8,128)}, u32[]{:S(2)}) copy-start(f32[2,512,128,8]{2,1,3,0:T(8,128)} %get-tuple-element.203) | copy-start | bytes 12582916 | tf_op jit(solution)/shard_map/while
  223.7 3.4 %copy-start.1 = (f32[2,512,128,8]{2,1,3,0:T(8,128)S(1)}, f32[2,512,128,8]{2,1,3,0:T(8,128)}, u32[]{:S(2)}) copy-start(f32[2,512,128,8]{2,1,3,0:T(8,128)} %get-tuple-element.203) | copy-start | bytes 12582916 | tf_op jit(solution)/shard_map/while
  234.9 3.4 %copy-start.1 = (f32[2,512,128,8]{2,1,3,0:T(8,128)S(1)}, f32[2,512,128,8]{2,1,3,0:T(8,128)}, u32[]{:S(2)}) copy-start(f32[2,512,128,8]{2,1,3,0:T(8,128)} %get-tuple-element.203) | copy-start | bytes 12582916 | tf_op jit(solution)/shard_map/while
  246.1 3.4 %copy-start.1 = (f32[2,512,128,8]{2,1,3,0:T(8,128)S(1)}, f32[2,512,128,8]{2,1,3,0:T(8,128)}, u32[]{:S(2)}) copy-start(f32[2,512,128,8]{2,1,3,0:T(8,128)} %get-tuple-element.203) | copy-start | bytes 12582916 | tf_op jit(solution)/shard_map/while
  257.3 3.4 %copy-start.1 = (f32[2,512,128,8]{2,1,3,0:T(8,128)S(1)}, f32[2,512,128,8]{2,1,3,0:T(8,128)}, u32[]{:S(2)}) copy-start(f32[2,512,128,8]{2,1,3,0:T(8,128)} %get-tuple-element.203) | copy-start | bytes 12582916 | tf_op jit(solution)/shard_map/while
  268.5 3.4 %copy-start.1 = (f32[2,512,128,8]{2,1,3,0:T(8,128)S(1)}, f32[2,512,128,8]{2,1,3,0:T(8,128)}, u32[]{:S(2)}) copy-start(f32[2,512,128,8]{2,1,3,0:T(8,128)} %get-tuple-element.203) | copy-start | bytes 12582916 | tf_op jit(solution)/shard_map/while
  279.7 3.4 %copy-start.1 = (f32[2,512,128,8]{2,1,3,0:T(8,128)S(1)}, f32[2,512,128,8]{2,1,3,0:T(8,128)}, u32[]{:S(2)}) copy-start(f32[2,512,128,8]{2,1,3,0:T(8,128)} %get-tuple-element.203) | copy-start | bytes 12582916 | tf_op jit(solution)/shard_map/while
  290.9 3.4 %copy-start.1 = (f32[2,512,128,8]{2,1,3,0:T(8,128)S(1)}, f32[2,512,128,8]{2,1,3,0:T(8,128)}, u32[]{:S(2)}) copy-start(f32[2,512,128,8]{2,1,3,0:T(8,128)} %get-tuple-element.203) | copy-start | bytes 12582916 | tf_op jit(solution)/shard_map/while
Sparse Core Ops, SparseCore 0:
  34.1 84.8 all-gather.2
  122.8 84.6 all-gather.4
where the time goes:
time: 311 us; the launch traced here: 310 us
  waiting for transfers between devices  124 us (40%)
  matrix products  60 us (19%)
  other arithmetic  41.4 us (13%)
  starting transfers between devices  34.9 us (11%)
  local copies, waits for them, and re-layouts  29.7 us (10%)
  between operations  14.4 us (5%)
  loops' own time  5.69 us (2%)
    all_to_all x1, waiting for transfers between devices, local(): lax.all_to_all(partials.astype(jnp.bfloat16), 'exp', split_axis=0, concat...  43 us
    all_to_all x1, waiting for transfers between devices, local(): lax.all_to_all(spread_rows, 'exp', split_axis=0, concat_axis=0, tiled=True)  36.6 us
    dot_general x8, matrix products, advance(): jnp.einsum('qhgd,khd->hgqk', grouped, key_block, preferred_element_type=j...  29.5 us
    all_to_all x1, waiting for transfers between devices, local(): lax.all_to_all(outgoing, 'ctx', split_axis=1, concat_axis=1, tiled=True)  27.4 us
    reduce_sum x8, other arithmetic, advance(): totals = totals * factor + jnp.sum(weights, axis=-1)  26.6 us
    dot_general x8, matrix products, advance(): jnp.einsum('hgqk,khd->hgqd', weights.astype(jnp.bfloat16), value_block, p...  21.1 us
    all_gather x1, waiting for transfers between devices, attention(): value_piece = lax.all_gather(value_rows, 'ctx', axis=1, tiled=True)  14.3 us
    all_to_all x1, starting transfers between devices, local(): lax.all_to_all(outgoing, 'ctx', split_axis=1, concat_axis=1, tiled=True)  13.2 us
  transfers between devices with their start and end apart: 7, of which 5 were waited for; matrix products, arithmetic and copies ran while one was open for 38% of the time, Pallas kernels for 0%

commit v1 on v0

--- a/solution.py
+++ b/solution.py
@@ -3,6 +3,15 @@
 import jax.numpy as jnp
 from jax import lax
 from jax.sharding import PartitionSpec as P
+
+
+def process_digits_for(x0):
+    r2 = lax.axis_size("ctx")
+    back = jnp.split(x0, r2, axis=1)
+    opened = jnp.stack(back)
+    part_next = lax.all_to_all(opened, "ctx", 0, 0)
+    x_next = jnp.concatenate(part_next, 1)
+    return x_next
 
 
 def from_partner(value, axis, bit):
@@ -118,7 +127,7 @@
         jnp.zeros((expert_total * capacity, features), jnp.bfloat16).at[target].set(source_rows)
     )
     outgoing = outgoing.reshape(per_ctx, ctx_count, capacity, features)
-    arrived = lax.all_to_all(outgoing, "ctx", split_axis=1, concat_axis=1, tiled=True)
+    arrived = process_digits_for(outgoing)
     stacked = jnp.stack([gate_weight, up_weight, down_weight], axis=0)
     my_exp = lax.axis_index("exp")
     partner = from_partner(stacked, "exp", 0)

time: 311 us -> 329 us (1.058)
  the two profiles are of different devices: /device:TPU:16 before, /device:TPU:8 now
where the time goes in v1:
time: 329 us; the launch traced here: 327 us
  waiting for transfers between devices  123 us (37%)
  matrix products  59.4 us (18%)
  local copies, waits for them, and re-layouts  48.3 us (15%)
  other arithmetic  41.4 us (13%)
  starting transfers between devices  35 us (11%)
  between operations  14.4 us (4%)
  loops' own time  5.69 us (2%)
    all_to_all x1, waiting for transfers between devices, local(): lax.all_to_all(partials.astype(jnp.bfloat16), 'exp', split_axis=0, concat...  43 us
    all_to_all x1, waiting for transfers between devices, local(): lax.all_to_all(spread_rows, 'exp', split_axis=0, concat_axis=0, tiled=True)  36.6 us
    dot_general x8, matrix products, advance(): jnp.einsum('qhgd,khd->hgqk', grouped, key_block, preferred_element_type=j...  28.9 us
    all_to_all x1, waiting for transfers between devices, process_digits_for(): part_next = lax.all_to_all(opened, 'ctx', 0, 0)  27.4 us
    reduce_sum x8, other arithmetic, advance(): totals = totals * factor + jnp.sum(weights, axis=-1)  26.6 us
    unnamed x54, local copies, waits for them, and re-layouts  22.6 us
    dot_general x8, matrix products, advance(): jnp.einsum('hgqk,khd->hgqd', weights.astype(jnp.bfloat16), value_block, p...  21.1 us
    all_gather x1, waiting for transfers between devices, attention(): value_piece = lax.all_gather(value_rows, 'ctx', axis=1, tiled=True)  14 us
  transfers between devices with their start and end apart: 7, of which 5 were waited for; matrix products, arithmetic and copies ran while one was open for 36% of the time, Pallas kernels for 0%

profile of v1, /device:TPU:8, one launch (start us, length us, event | category | flops | bytes accessed | tf_op | source)
XLA Modules:
  0.0 327.4 jit_solution(14878235149718933328)
XLA Ops:
  12.4 1.9 scatter_custom_fusion
  34.7 13.2 %all-to-all-start = ((bf16[32,4,1,4,1024]{4,3,1,2,0:T(4,128)(2,1)}), bf16[32,4,1,4,1024]{4,3,1,2,0:T(4,128)(2,1)S(1)}, u32[]{:S(2)}, u32[]{:S(2)}) async-start(bf16[32,4,1,4,1024]{4,3,1,2,0:T(4,128)(2,1)} %constant_dynamic-update-slice_fusion), calls=%async_computation | async-start | bytes 2097152 | tf_op jit(solution)/shard_map/all_to_all | solution.py:12
  48.6 27.4 %all-to-all-done = bf16[32,4,1,4,1024]{4,3,1,2,0:T(4,128)(2,1)S(1)} async-done(((bf16[32,4,1,4,1024]{4,3,1,2,0:T(4,128)(2,1)}), bf16[32,4,1,4,1024]{4,3,1,2,0:T(4,128)(2,1)S(1)}, u32[]{:S(2)}, u32[]{:S(2)}) %all-to-all-start) | async-done | bytes 1048608 | tf_op jit(solution)/shard_map/all_to_all | solution.py:12
  76.4 2.2 broadcast_in_dim.66
  78.6 7.7 %all-to-all-start.1 = ((bf16[16,16,4,1024]{3,2,1,0:T(4,128)(2,1)}), bf16[16,16,4,1024]{3,2,1,0:T(4,128)(2,1)S(1)}, u32[]{:S(2)}, u32[]{:S(2)}) async-start(bf16[16,16,4,1024]{3,2,1,0:T(4,128)(2,1)} %bitcast.312), calls=%async_computation.1 | async-start | bytes 4194304 | tf_op jit(solution)/shard_map/all_to_all | solution.py:146
  86.4 2.1 pad_maximum_fusion
  88.5 2.0 collective-permute-start
  91.3 2.3 collective-permute-done
  93.6 3.5 %maximum_select_fusion = bf16[3,384,1024]{2,1,0:T(8,128)(2,1)} fusion(bf16[1,192,1024]{2,1,0:T(8,128)(2,1)S(1)} %bitcast.316, bf16[1,192,1024]{2,1,0:T(8,128)(2,1)S(1)} %bitcast.318, bf16[1,192,1024]{2,1,0:T(8,128)(2,1)} %bitcast.320, bf16[3,192,1024]{2,1,0:T(8,128)(2,1)} %collective-permute-done, pred[]{:T(512)S(6)} %eq.35), kind=kLoop, calls=%fused_computation.30 | loop fusion | flops 20054016 | bytes 4718593 | tf_op jit(solution)/shard_map/jit(_where)/select_n | solution.py:135
  97.1 36.6 %all-to-all-done.1 = bf16[16,16,4,1024]{3,2,1,0:T(4,128)(2,1)S(1)} async-done(((bf16[16,16,4,1024]{3,2,1,0:T(4,128)(2,1)}), bf16[16,16,4,1024]{3,2,1,0:T(4,128)(2,1)S(1)}, u32[]{:S(2)}, u32[]{:S(2)}) %all-to-all-start.1) | async-done | bytes 2097184 | tf_op jit(solution)/shard_map/all_to_all | solution.py:146
  133.7 2.1 reshape.287
  135.8 3.2 fusion.22
  139.0 2.2 multiply_convert_fusion
  141.2 2.4 dot_general.22
  143.6 3.7 %convolution_convert_fusion = bf16[16,16,4,1024]{3,1,2,0:T(8,128)(2,1)} fusion(bf16[3,384,1024]{2,1,0:T(8,128)(2,1)S(1)} %copy-done.2, bf16[16,16,4,384]{3,2,1,0:T(4,128)(2,1)} %dot_general.22), kind=kOutput, calls=%fused_computation.31 | convolution fusion | flops 806354944 | bytes 3670016 | tf_op jit(solution)/shard_map/dot_general | solution.py:28
  147.3 6.7 %all-to-all-start.2 = ((bf16[16,16,4,1024]{3,1,2,0:T(8,128)(2,1)}), bf16[16,16,4,1024]{3,1,2,0:T(8,128)(2,1)S(1)}, u32[]{:S(2)}, u32[]{:S(2)}) async-start(bf16[16,16,4,1024]{3,1,2,0:T(8,128)(2,1)} %convolution_convert_fusion), calls=%async_computation.2 | async-start | bytes 4194304 | tf_op jit(solution)/shard_map/all_to_all | solution.py:148
  156.1 1.9 gather_fusion.1
  158.4 43.0 %all-to-all-done.2 = bf16[16,16,4,1024]{3,1,2,0:T(8,128)(2,1)S(1)} async-done(((bf16[16,16,4,1024]{3,1,2,0:T(8,128)(2,1)}), bf16[16,16,4,1024]{3,1,2,0:T(8,128)(2,1)S(1)}, u32[]{:S(2)}, u32[]{:S(2)}) %all-to-all-start.2) | async-done | bytes 2097184 | tf_op jit(solution)/shard_map/all_to_all | solution.py:148
  201.4 1.8 reduce
  204.5 1.9 copy.243
  206.4 5.3 %all-to-all-start.3 = ((bf16[4,32,4,1024]{3,2,0,1:T(4,128)(2,1)}), bf16[4,32,4,1024]{3,2,0,1:T(4,128)(2,1)S(1)}, u32[]{:S(2)}, u32[]{:S(2)}) async-start(bf16[4,32,4,1024]{3,2,0,1:T(4,128)(2,1)} %copy.243), calls=%async_computation.3 | async-start | bytes 2097152 | tf_op jit(solution)/shard_map/all_to_all | solution.py:155
  211.7 14.0 %all-gather.5.cloned.1.call-done = bf16[1,4096,2,128]{3,1,2,0:T(8,128)(2,1)} async-done(((bf16[1,128,2,128]{3,1,2,0:T(8,128)(2,1)}), bf16[1,4096,2,128]{3,1,2,0:T(8,128)(2,1)}) %all-gather.5.cloned.1.call-update) | async-done | bytes 2097168 | tf_op jit(solution)/shard_map/all_gather | solution.py:47
  225.7 89.0 %while.15 = (s32[]{:T(128)}, f32[2,8,128]{2,1,0:T(8,128)S(1)}, f32[2,8,128]{2,1,0:T(8,128)S(1)}, f32[2,8,128,128]{3,2,1,0:T(8,128)S(1)}, s32[8]{0:T(128)S(1)}, /...) while((s32[]{:T(128)}, f32[2,8,128]{2,1,0:T(8,128)S(1)}, ...), condition=%wide.region_3.4_spmd.clone, body=%wide.region_0.3_spmd.clone.sunk | while | flops 551365248 | bytes 32904396 | solution.py:76
  227.1 3.6 %fusion.58 = (f32[2,8,128]{2,1,0:T(8,128)S(1)}, f32[2,512,128,8]{2,1,3,0:T(8,128)}) fusion(pred[128,512]{0,1:T(8,128)(4,1)S(1)} %broadcast_compare_fusion.2, bf16[128,2,8,128]{3,0,2,1:T(8,128)(2,1)S(1)} %get-tuple-element.236, bf16[8,512,2,128]{3,1,0,2:T(8,128)(2,1)} %get-tuple-element.235, s32[]{:T(128)S(6)} %copy.293), kind=kOutput, calls=%fused_computation.6.clone.1 | convolution fusion | flops 271579136 | bytes 5054468 | tf_op jit(solution)/shard_map/while/body/eval_jaxpr/qhgd,khd->hgqk/dot_general | solution.py:58
  230.7 3.3 %fusion.59 = f32[2,8,128]{2,1,0:T(8,128)S(1)} fusion(f32[2,512,128,8]{2,1,3,0:T(8,128)} %get-tuple-element.203, f32[2,8,128]{2,1,0:T(8,128)S(1)} %select_maximum_fusion.2, pred[128,512]{0,1:T(8,128)(4,1)S(1)} %broadcast_compare_fusion.2), kind=kLoop, calls=%fused_computation.8.clone.1 | loop fusion | flops 5240832 | bytes 4276224 | tf_op jit(solution)/shard_map/while/body/eval_jaxpr/reduce_sum | solution.py:67
  234.1 2.6 fusion.61
  238.2 3.6 %fusion.58 = (f32[2,8,128]{2,1,0:T(8,128)S(1)}, f32[2,512,128,8]{2,1,3,0:T(8,128)}) fusion(pred[128,512]{0,1:T(8,128)(4,1)S(1)} %broadcast_compare_fusion.2, bf16[128,2,8,128]{3,0,2,1:T(8,128)(2,1)S(1)} %get-tuple-element.236, bf16[8,512,2,128]{3,1,0,2:T(8,128)(2,1)} %get-tuple-element.235, s32[]{:T(128)S(6)} %copy.293), kind=kOutput, calls=%fused_computation.6.clone.1 | convolution fusion | flops 271579136 | bytes 5054468 | tf_op jit(solution)/shard_map/while/body/eval_jaxpr/qhgd,khd->hgqk/dot_general | solution.py:58
  241.8 3.3 %fusion.59 = f32[2,8,128]{2,1,0:T(8,128)S(1)} fusion(f32[2,512,128,8]{2,1,3,0:T(8,128)} %get-tuple-element.203, f32[2,8,128]{2,1,0:T(8,128)S(1)} %select_maximum_fusion.2, pred[128,512]{0,1:T(8,128)(4,1)S(1)} %broadcast_compare_fusion.2), kind=kLoop, calls=%fused_computation.8.clone.1 | loop fusion | flops 5240832 | bytes 4276224 | tf_op jit(solution)/shard_map/while/body/eval_jaxpr/reduce_sum | solution.py:67
  245.3 2.6 fusion.61
  249.3 3.6 %fusion.58 = (f32[2,8,128]{2,1,0:T(8,128)S(1)}, f32[2,512,128,8]{2,1,3,0:T(8,128)}) fusion(pred[128,512]{0,1:T(8,128)(4,1)S(1)} %broadcast_compare_fusion.2, bf16[128,2,8,128]{3,0,2,1:T(8,128)(2,1)S(1)} %get-tuple-element.236, bf16[8,512,2,128]{3,1,0,2:T(8,128)(2,1)} %get-tuple-element.235, s32[]{:T(128)S(6)} %copy.293), kind=kOutput, calls=%fused_computation.6.clone.1 | convolution fusion | flops 271579136 | bytes 5054468 | tf_op jit(solution)/shard_map/while/body/eval_jaxpr/qhgd,khd->hgqk/dot_general | solution.py:58
  253.0 3.3 %fusion.59 = f32[2,8,128]{2,1,0:T(8,128)S(1)} fusion(f32[2,512,128,8]{2,1,3,0:T(8,128)} %get-tuple-element.203, f32[2,8,128]{2,1,0:T(8,128)S(1)} %select_maximum_fusion.2, pred[128,512]{0,1:T(8,128)(4,1)S(1)} %broadcast_compare_fusion.2), kind=kLoop, calls=%fused_computation.8.clone.1 | loop fusion | flops 5240832 | bytes 4276224 | tf_op jit(solution)/shard_map/while/body/eval_jaxpr/reduce_sum | solution.py:67
  256.4 2.6 fusion.61
  260.5 3.6 %fusion.58 = (f32[2,8,128]{2,1,0:T(8,128)S(1)}, f32[2,512,128,8]{2,1,3,0:T(8,128)}) fusion(pred[128,512]{0,1:T(8,128)(4,1)S(1)} %broadcast_compare_fusion.2, bf16[128,2,8,128]{3,0,2,1:T(8,128)(2,1)S(1)} %get-tuple-element.236, bf16[8,512,2,128]{3,1,0,2:T(8,128)(2,1)} %get-tuple-element.235, s32[]{:T(128)S(6)} %copy.293), kind=kOutput, calls=%fused_computation.6.clone.1 | convolution fusion | flops 271579136 | bytes 5054468 | tf_op jit(solution)/shard_map/while/body/eval_jaxpr/qhgd,khd->hgqk/dot_general | solution.py:58
  264.1 3.3 %fusion.59 = f32[2,8,128]{2,1,0:T(8,128)S(1)} fusion(f32[2,512,128,8]{2,1,3,0:T(8,128)} %get-tuple-element.203, f32[2,8,128]{2,1,0:T(8,128)S(1)} %select_maximum_fusion.2, pred[128,512]{0,1:T(8,128)(4,1)S(1)} %broadcast_compare_fusion.2), kind=kLoop, calls=%fused_computation.8.clone.1 | loop fusion | flops 5240832 | bytes 4276224 | tf_op jit(solution)/shard_map/while/body/eval_jaxpr/reduce_sum | solution.py:67
  267.5 2.6 fusion.61
  271.6 3.6 %fusion.58 = (f32[2,8,128]{2,1,0:T(8,128)S(1)}, f32[2,512,128,8]{2,1,3,0:T(8,128)}) fusion(pred[128,512]{0,1:T(8,128)(4,1)S(1)} %broadcast_compare_fusion.2, bf16[128,2,8,128]{3,0,2,1:T(8,128)(2,1)S(1)} %get-tuple-element.236, bf16[8,512,2,128]{3,1,0,2:T(8,128)(2,1)} %get-tuple-element.235, s32[]{:T(128)S(6)} %copy.293), kind=kOutput, calls=%fused_computation.6.clone.1 | convolution fusion | flops 271579136 | bytes 5054468 | tf_op jit(solution)/shard_map/while/body/eval_jaxpr/qhgd,khd->hgqk/dot_general | solution.py:58
  275.2 3.3 %fusion.59 = f32[2,8,128]{2,1,0:T(8,128)S(1)} fusion(f32[2,512,128,8]{2,1,3,0:T(8,128)} %get-tuple-element.203, f32[2,8,128]{2,1,0:T(8,128)S(1)} %select_maximum_fusion.2, pred[128,512]{0,1:T(8,128)(4,1)S(1)} %broadcast_compare_fusion.2), kind=kLoop, calls=%fused_computation.8.clone.1 | loop fusion | flops 5240832 | bytes 4276224 | tf_op jit(solution)/shard_map/while/body/eval_jaxpr/reduce_sum | solution.py:67
  278.7 2.6 fusion.61
  282.7 3.6 %fusion.58 = (f32[2,8,128]{2,1,0:T(8,128)S(1)}, f32[2,512,128,8]{2,1,3,0:T(8,128)}) fusion(pred[128,512]{0,1:T(8,128)(4,1)S(1)} %broadcast_compare_fusion.2, bf16[128,2,8,128]{3,0,2,1:T(8,128)(2,1)S(1)} %get-tuple-element.236, bf16[8,512,2,128]{3,1,0,2:T(8,128)(2,1)} %get-tuple-element.235, s32[]{:T(128)S(6)} %copy.293), kind=kOutput, calls=%fused_computation.6.clone.1 | convolution fusion | flops 271579136 | bytes 5054468 | tf_op jit(solution)/shard_map/while/body/eval_jaxpr/qhgd,khd->hgqk/dot_general | solution.py:58
  286.3 3.3 %fusion.59 = f32[2,8,128]{2,1,0:T(8,128)S(1)} fusion(f32[2,512,128,8]{2,1,3,0:T(8,128)} %get-tuple-element.203, f32[2,8,128]{2,1,0:T(8,128)S(1)} %select_maximum_fusion.2, pred[128,512]{0,1:T(8,128)(4,1)S(1)} %broadcast_compare_fusion.2), kind=kLoop, calls=%fused_computation.8.clone.1 | loop fusion | flops 5240832 | bytes 4276224 | tf_op jit(solution)/shard_map/while/body/eval_jaxpr/reduce_sum | solution.py:67
  289.8 2.6 fusion.61
  293.9 3.6 %fusion.58 = (f32[2,8,128]{2,1,0:T(8,128)S(1)}, f32[2,512,128,8]{2,1,3,0:T(8,128)}) fusion(pred[128,512]{0,1:T(8,128)(4,1)S(1)} %broadcast_compare_fusion.2, bf16[128,2,8,128]{3,0,2,1:T(8,128)(2,1)S(1)} %get-tuple-element.236, bf16[8,512,2,128]{3,1,0,2:T(8,128)(2,1)} %get-tuple-element.235, s32[]{:T(128)S(6)} %copy.293), kind=kOutput, calls=%fused_computation.6.clone.1 | convolution fusion | flops 271579136 | bytes 5054468 | tf_op jit(solution)/shard_map/while/body/eval_jaxpr/qhgd,khd->hgqk/dot_general | solution.py:58
  297.5 3.3 %fusion.59 = f32[2,8,128]{2,1,0:T(8,128)S(1)} fusion(f32[2,512,128,8]{2,1,3,0:T(8,128)} %get-tuple-element.203, f32[2,8,128]{2,1,0:T(8,128)S(1)} %select_maximum_fusion.2, pred[128,512]{0,1:T(8,128)(4,1)S(1)} %broadcast_compare_fusion.2), kind=kLoop, calls=%fused_computation.8.clone.1 | loop fusion | flops 5240832 | bytes 4276224 | tf_op jit(solution)/shard_map/while/body/eval_jaxpr/reduce_sum | solution.py:67
  300.9 2.6 fusion.61
  305.0 3.6 %fusion.58 = (f32[2,8,128]{2,1,0:T(8,128)S(1)}, f32[2,512,128,8]{2,1,3,0:T(8,128)}) fusion(pred[128,512]{0,1:T(8,128)(4,1)S(1)} %broadcast_compare_fusion.2, bf16[128,2,8,128]{3,0,2,1:T(8,128)(2,1)S(1)} %get-tuple-element.236, bf16[8,512,2,128]{3,1,0,2:T(8,128)(2,1)} %get-tuple-element.235, s32[]{:T(128)S(6)} %copy.293), kind=kOutput, calls=%fused_computation.6.clone.1 | convolution fusion | flops 271579136 | bytes 5054468 | tf_op jit(solution)/shard_map/while/body/eval_jaxpr/qhgd,khd->hgqk/dot_general | solution.py:58
  308.6 3.3 %fusion.59 = f32[2,8,128]{2,1,0:T(8,128)S(1)} fusion(f32[2,512,128,8]{2,1,3,0:T(8,128)} %get-tuple-element.203, f32[2,8,128]{2,1,0:T(8,128)S(1)} %select_maximum_fusion.2, pred[128,512]{0,1:T(8,128)(4,1)S(1)} %broadcast_compare_fusion.2), kind=kLoop, calls=%fused_computation.8.clone.1 | loop fusion | flops 5240832 | bytes 4276224 | tf_op jit(solution)/shard_map/while/body/eval_jaxpr/reduce_sum | solution.py:67
  312.0 2.6 fusion.61
  318.3 2.3 multiply_reduce_fusion
  (177 shorter events, 41.4 us)
Async XLA Ops:
  7.2 148.7 %copy-start = (bf16[1024,128]{1,0:T(8,128)(2,1)S(1)}, bf16[1024,128]{1,0:T(8,128)(2,1)}, u32[]{:S(2)}) copy-start(bf16[1024,128]{1,0:T(8,128)(2,1)} %param.18) | copy-start | bytes 786436
  14.8 33.2 %copy-start.7 = (bf16[1,128,2,128]{3,2,1,0:T(2,128)(2,1)S(1)}, bf16[1,128,2,128]{3,2,1,0:T(2,128)(2,1)}, u32[]{:S(2)}) copy-start(bf16[1,128,2,128]{3,2,1,0:T(2,128)(2,1)} %param.14) | copy-start | bytes 196612
  34.7 41.3 %all-to-all-start = ((bf16[32,4,1,4,1024]{4,3,1,2,0:T(4,128)(2,1)}), bf16[32,4,1,4,1024]{4,3,1,2,0:T(4,128)(2,1)S(1)}, u32[]{:S(2)}, u32[]{:S(2)}) async-start(bf16[32,4,1,4,1024]{4,3,1,2,0:T(4,128)(2,1)} %constant_dynamic-update-slice_fusion), calls=%async_computation | async-start | bytes 2097152 | tf_op jit(solution)/shard_map/all_to_all | solution.py:12
  47.9 163.8 %all-gather.3.cloned.1.call-start = ((), (), s32[]{:S(2)}) async-start(), calls=%async_computation.4 | async-start | bytes 2162688 | tf_op jit(solution)/shard_map/all_gather | solution.py:46
  78.6 7.8 %copy-start.4 = (bf16[192,1024]{1,0:T(8,128)(2,1)S(1)}, bf16[192,1024]{1,0:T(8,128)(2,1)}, u32[]{:S(2)}) copy-start(bf16[192,1024]{1,0:T(8,128)(2,1)} %param.21) | copy-start | bytes 1179652
  78.6 7.8 %copy-start.5 = (bf16[192,1024]{1,0:T(8,128)(2,1)S(1)}, bf16[192,1024]{1,0:T(8,128)(2,1)}, u32[]{:S(2)}) copy-start(bf16[192,1024]{1,0:T(8,128)(2,1)} %param.20) | copy-start | bytes 1179652
  78.6 12.0 %copy-start.8 = (bf16[1,128,2,128]{3,2,1,0:T(2,128)(2,1)S(1)}, bf16[1,128,2,128]{3,2,1,0:T(2,128)(2,1)}, u32[]{:S(2)}) copy-start(bf16[1,128,2,128]{3,2,1,0:T(2,128)(2,1)} %param.15) | copy-start | bytes 196612
  78.6 55.1 %all-to-all-start.1 = ((bf16[16,16,4,1024]{3,2,1,0:T(4,128)(2,1)}), bf16[16,16,4,1024]{3,2,1,0:T(4,128)(2,1)S(1)}, u32[]{:S(2)}, u32[]{:S(2)}) async-start(bf16[16,16,4,1024]{3,2,1,0:T(4,128)(2,1)} %bitcast.312), calls=%async_computation.1 | async-start | bytes 4194304 | tf_op jit(solution)/shard_map/all_to_all | solution.py:146
  86.3 139.4 %all-gather.5.cloned.1.call-start = ((), (), s32[]{:S(2)}) async-start(), calls=%async_computation.5 | async-start | bytes 2162688 | tf_op jit(solution)/shard_map/all_gather | solution.py:47
  88.5 5.1 %collective-permute-start = (bf16[3,192,1024]{2,1,0:T(8,128)(2,1)}, bf16[3,192,1024]{2,1,0:T(8,128)(2,1)}, u32[]{:S(2)}, u32[]{:S(2)}) collective-permute-start(bf16[3,192,1024]{2,1,0:T(8,128)(2,1)} %pad_maximum_fusion), channel_id=1, source_target_pairs={{0,1},{1,0},{2,3},{3,2},{4,5},{5,4},{6,7},{7,6},{8,9},{9,8},{10,11... | collective-permute-start | bytes 3538952 | tf_op jit(solution)/shard_map/ppermute | solution.py:18
  135.8 3.2 copy-start.2
  135.8 3.2 copy-start.3
  147.3 8.1 %copy-start.9 = (s32[1,128,2]{1,2,0:T(2,128)S(1)}, s32[1,128,2]{1,2,0:T(2,128)}, u32[]{:S(2)}) copy-start(s32[1,128,2]{1,2,0:T(2,128)} %param.16) | copy-start | bytes 3076
  147.3 54.1 %all-to-all-start.2 = ((bf16[16,16,4,1024]{3,1,2,0:T(8,128)(2,1)}), bf16[16,16,4,1024]{3,1,2,0:T(8,128)(2,1)S(1)}, u32[]{:S(2)}, u32[]{:S(2)}) async-start(bf16[16,16,4,1024]{3,1,2,0:T(8,128)(2,1)} %convolution_convert_fusion), calls=%async_computation.2 | async-start | bytes 4194304 | tf_op jit(solution)/shard_map/all_to_all | solution.py:148
  204.5 21.2 %copy-start.6 = (f32[2,8,128,128]{3,2,1,0:T(8,128)S(1)}, f32[2,8,128,128]{3,2,1,0:T(8,128)}, u32[]{:S(2)}) copy-start(f32[2,8,128,128]{3,2,1,0:T(8,128)} %custom-call.4) | copy-start | bytes 3145732
  206.4 109.8 %all-to-all-start.3 = ((bf16[4,32,4,1024]{3,2,0,1:T(4,128)(2,1)}), bf16[4,32,4,1024]{3,2,0,1:T(4,128)(2,1)S(1)}, u32[]{:S(2)}, u32[]{:S(2)}) async-start(bf16[4,32,4,1024]{3,2,0,1:T(4,128)(2,1)} %copy.243), calls=%async_computation.3 | async-start | bytes 2097152 | tf_op jit(solution)/shard_map/all_to_all | solution.py:155
  230.7 3.4 %copy-start.1 = (f32[2,512,128,8]{2,1,3,0:T(8,128)S(1)}, f32[2,512,128,8]{2,1,3,0:T(8,128)}, u32[]{:S(2)}) copy-start(f32[2,512,128,8]{2,1,3,0:T(8,128)} %get-tuple-element.203) | copy-start | bytes 12582916 | tf_op jit(solution)/shard_map/while
  241.8 3.4 %copy-start.1 = (f32[2,512,128,8]{2,1,3,0:T(8,128)S(1)}, f32[2,512,128,8]{2,1,3,0:T(8,128)}, u32[]{:S(2)}) copy-start(f32[2,512,128,8]{2,1,3,0:T(8,128)} %get-tuple-element.203) | copy-start | bytes 12582916 | tf_op jit(solution)/shard_map/while
  252.9 3.4 %copy-start.1 = (f32[2,512,128,8]{2,1,3,0:T(8,128)S(1)}, f32[2,512,128,8]{2,1,3,0:T(8,128)}, u32[]{:S(2)}) copy-start(f32[2,512,128,8]{2,1,3,0:T(8,128)} %get-tuple-element.203) | copy-start | bytes 12582916 | tf_op jit(solution)/shard_map/while
  264.1 3.4 %copy-start.1 = (f32[2,512,128,8]{2,1,3,0:T(8,128)S(1)}, f32[2,512,128,8]{2,1,3,0:T(8,128)}, u32[]{:S(2)}) copy-start(f32[2,512,128,8]{2,1,3,0:T(8,128)} %get-tuple-element.203) | copy-start | bytes 12582916 | tf_op jit(solution)/shard_map/while
  275.2 3.4 %copy-start.1 = (f32[2,512,128,8]{2,1,3,0:T(8,128)S(1)}, f32[2,512,128,8]{2,1,3,0:T(8,128)}, u32[]{:S(2)}) copy-start(f32[2,512,128,8]{2,1,3,0:T(8,128)} %get-tuple-element.203) | copy-start | bytes 12582916 | tf_op jit(solution)/shard_map/while
  286.3 3.4 %copy-start.1 = (f32[2,512,128,8]{2,1,3,0:T(8,128)S(1)}, f32[2,512,128,8]{2,1,3,0:T(8,128)}, u32[]{:S(2)}) copy-start(f32[2,512,128,8]{2,1,3,0:T(8,128)} %get-tuple-element.203) | copy-start | bytes 12582916 | tf_op jit(solution)/shard_map/while
  297.5 3.4 %copy-start.1 = (f32[2,512,128,8]{2,1,3,0:T(8,128)S(1)}, f32[2,512,128,8]{2,1,3,0:T(8,128)}, u32[]{:S(2)}) copy-start(f32[2,512,128,8]{2,1,3,0:T(8,128)} %get-tuple-element.203) | copy-start | bytes 12582916 | tf_op jit(solution)/shard_map/while
  308.6 3.4 %copy-start.1 = (f32[2,512,128,8]{2,1,3,0:T(8,128)S(1)}, f32[2,512,128,8]{2,1,3,0:T(8,128)}, u32[]{:S(2)}) copy-start(f32[2,512,128,8]{2,1,3,0:T(8,128)} %get-tuple-element.203) | copy-start | bytes 12582916 | tf_op jit(solution)/shard_map/while
Sparse Core Ops, SparseCore 0:
  52.5 85.1 all-gather.2
  141.4 84.2 all-gather.4
